TPU v7x, 512 devices: a whole 4x8x8 slice. The times are simulated.
512 devices in a mesh: dp: 128 (over y, z, core), tp: 4 (over x).
Axes of the slice: x: 4, y: 8, z: 8, core: 2. Of those that a mesh axis runs over, the one named last changes fastest.
Arguments:
- hidden: bfloat16 [2048, 2048], P('dp'), may hold values from -6 to 6
- routes: int32 [2048, 8], P('dp'), may hold values from 0 to 127, all different within a row; in each aligned block of 16 rows (0 to 15, 16 to 31, ...) at most 2 rows name the same one
- route_weights: int32 [2048, 8], P('dp'), may hold values from 1 to 65535
- w_gate: bfloat16 [128, 2048, 1024], P('dp', None, 'tp'), may hold values from -0.125 to 0.125
- w_up: bfloat16 [128, 2048, 1024], P('dp', None, 'tp'), may hold values from -0.125 to 0.125
- w_down: bfloat16 [128, 1024, 2048], P('dp', 'tp'), may hold values from -0.1875 to 0.1875
- queries: bfloat16 [1024, 8192], P('dp', 'tp'), may hold values from -480 to 480
- key_codes: bfloat16 [262144, 512], P('dp', 'tp'), may hold values from -127 to 127, as said below
- key_scales: float32 [4, 262144], P('tp', 'dp'), may hold values from 0.004 to 0.02
- cache_values: bfloat16 [262144, 512], P('dp', 'tp'), may hold values from -6 to 6
- new_keys: bfloat16 [1024, 512], P('dp', 'tp'), may hold values from -6 to 6
- new_values: bfloat16 [1024, 512], P('dp', 'tp'), may hold values from -6 to 6
- lengths: int32 [1024], P('dp'), may hold values from 1 to 2041, as said below
Outputs:
- expert_mix: bfloat16 [2048, 2048], P('dp')
- attended: bfloat16 [1024, 8192], P('dp', 'tp')
Inputs may be any that keep to these rules, and one draw needn't show every extreme that they name: `lengths`: the 8 requests of each block sum to at most 2048 positions; in every draw some block sums to exactly 2048, one of its requests holding 2048 - 7 positions. `routes`: each row names 8 different experts. Among the rows of one index of dp no expert is named more than 2 times, and in every draw some expert is named exactly 2 times by the rows of some index. `key_codes`: whole numbers.
All inputs are finite; a program needn't handle non-finite values.
Results may differ from a plain program's by a relative error of at most 0.014.
The roundings to bfloat16 on the way count: a program that leaves them out, or rounds other values in their place, can miss the bound.
Values may be sent and summed in bfloat16 or wider, within the bound.
No kernel may reach another device: no remote copies, remote signals or barrier semaphores. Data moves between devices by JAX's collectives and lax.ppermute only.
A program may use at most 64 MiB of HBM per device.

v0:
```python
import jax
import jax.numpy as jnp
from jax import lax
from jax.sharding import PartitionSpec as P

rope_base = 1000000.0


def inverse_freq(head_size):
    steps = jnp.arange(head_size // 2, dtype=jnp.float32) * (2.0 / head_size)
    return jnp.exp(-steps * jnp.log(jnp.float32(rope_base)))


def rotate(vector, angles):
    half_size = vector.shape[-1] // 2
    front_half = vector[..., :half_size]
    back_half = vector[..., half_size:]
    cosine = jnp.cos(angles)
    sine_part = jnp.sin(angles)
    return jnp.concatenate(
        [front_half * cosine - back_half * sine_part, back_half * cosine + front_half * sine_part],
        axis=-1,
    )


def attend_local(queries, codes, scales, cache_values, new_keys, new_values, lengths):
    row_count = queries.shape[0]
    cache_len = codes.shape[0]
    groups = scales.shape[0]
    head_size = codes.shape[1] // groups
    per_group = queries.shape[1] // (groups * head_size)
    request_end = jnp.cumsum(lengths)
    starts = request_end - lengths
    cache_pos = jnp.arange(cache_len, dtype=jnp.int32)
    member = (cache_pos[:, None] >= starts[None, :]) & (cache_pos[:, None] < request_end[None, :])
    offset = jnp.sum(jnp.where(member, starts[None, :], 0), axis=1)
    position = (cache_pos - offset).astype(jnp.float32)
    frequency = inverse_freq(head_size)
    cache_keys = (
        codes.astype(jnp.float32).reshape(cache_len, groups, head_size)
        * jnp.transpose(scales)[:, :, None]
    )
    cache_keys = rotate(cache_keys, position[:, None, None] * frequency[None, None, :]).astype(
        jnp.bfloat16
    )
    query_angles = lengths.astype(jnp.float32)[:, None] * frequency[None, :]
    rotated_query = queries.astype(jnp.float32).reshape(row_count, groups, per_group, head_size)
    rotated_query = rotate(rotated_query, query_angles[:, None, None, :]).astype(jnp.bfloat16)
    fresh_key = rotate(
        new_keys.astype(jnp.float32).reshape(row_count, groups, head_size), query_angles[:, None, :]
    ).astype(jnp.bfloat16)
    score_scale = head_size ** (-0.5)
    scores = (
        jnp.einsum("rgqd,cgd->rgqc", rotated_query, cache_keys, preferred_element_type=jnp.float32)
        * score_scale
    )
    own_score = (
        jnp.einsum("rgqd,rgd->rgq", rotated_query, fresh_key, preferred_element_type=jnp.float32)
        * score_scale
    )
    live_mask = jnp.transpose(member)[:, None, None, :]
    scores = jnp.where(live_mask, scores, -jnp.inf)
    peak_score = jnp.maximum(jnp.max(scores, axis=-1), own_score)
    weights = jnp.exp(scores - peak_score[..., None])
    own_weight = jnp.exp(own_score - peak_score)
    weight_sum = jnp.sum(weights, axis=-1) + own_weight
    value_rows = cache_values.reshape(cache_len, groups, head_size)
    mixture = jnp.einsum(
        "rgqc,cgd->rgqd",
        weights.astype(jnp.bfloat16),
        value_rows,
        preferred_element_type=jnp.float32,
    )
    mixture = mixture + own_weight[..., None] * new_values.astype(jnp.float32).reshape(
        row_count, groups, 1, head_size
    )
    return (
        (mixture / weight_sum[..., None])
        .reshape(row_count, groups * per_group * head_size)
        .astype(jnp.bfloat16)
    )


def expert_block(arrived, w_gate, w_up, w_down):
    arrived_shape = arrived.shape
    inputs = arrived.reshape(-1, arrived_shape[-1])
    gate_act = jnp.dot(inputs, w_gate[0], preferred_element_type=jnp.float32)
    up_act = jnp.dot(inputs, w_up[0], preferred_element_type=jnp.float32)
    hidden_act = (jax.nn.silu(gate_act) * up_act).astype(jnp.bfloat16)
    partial_value = jnp.dot(hidden_act, w_down[0], preferred_element_type=jnp.float32)
    return partial_value.reshape(arrived_shape[0], arrived_shape[1], partial_value.shape[-1])


def on_device(
    hidden,
    routes,
    route_weights,
    w_gate,
    w_up,
    w_down,
    queries,
    key_codes,
    key_scales,
    cache_values,
    new_keys,
    new_values,
    lengths,
):
    token_count = routes.shape[0]
    top_count = routes.shape[1]
    model_width = hidden.shape[1]
    tp_size = lax.axis_size("tp")
    dp_size = lax.axis_size("dp")
    slice_width = model_width // tp_size
    experts = dp_size * w_gate.shape[0]
    capacity = min(token_count, max(2, token_count * top_count * 2 // experts))
    flat_ids = routes.reshape(-1)
    onehot = (flat_ids[:, None] == jnp.arange(experts, dtype=jnp.int32)[None, :]).astype(jnp.int32)
    rank_ids = jnp.sum(onehot * (jnp.cumsum(onehot, axis=0) - 1), axis=1)
    slot_ids = flat_ids * capacity + rank_ids
    slot_grid = slot_ids.reshape(token_count, top_count)
    selector = jnp.any(
        jnp.arange(experts * capacity, dtype=jnp.int32)[:, None, None] == slot_grid[None, :, :],
        axis=2,
    ).astype(jnp.bfloat16)
    tp_index = lax.axis_index("tp")
    own_cols = lax.dynamic_slice_in_dim(hidden, tp_index * slice_width, slice_width, axis=1)
    outgoing = jnp.dot(selector, own_cols, preferred_element_type=jnp.float32).astype(jnp.bfloat16)
    outgoing = outgoing.reshape(experts, capacity, slice_width)
    arrived = lax.all_to_all(outgoing, "dp", split_axis=0, concat_axis=0, tiled=True)
    arrived = lax.all_gather(arrived, "tp", axis=0, tiled=False)
    slots = dp_size * capacity
    arrived = arrived.reshape(tp_size, slots, slice_width)
    gate_w = w_gate[0].reshape(tp_size, slice_width, w_gate.shape[2])
    up_w = w_up[0].reshape(tp_size, slice_width, w_up.shape[2])
    gate_act = jnp.einsum("tsd,tdh->sh", arrived, gate_w, preferred_element_type=jnp.float32)
    up_act = jnp.einsum("tsd,tdh->sh", arrived, up_w, preferred_element_type=jnp.float32)
    hidden_act = (jax.nn.silu(gate_act) * up_act).astype(jnp.bfloat16)
    partial_value = jnp.dot(hidden_act, w_down[0], preferred_element_type=jnp.float32)
    partial_value = partial_value.astype(jnp.bfloat16).reshape(slots, tp_size, slice_width)
    gathered = lax.all_to_all(partial_value, "tp", split_axis=1, concat_axis=1, tiled=True)
    expert_out = jnp.sum(gathered.astype(jnp.float32), axis=1).astype(jnp.bfloat16)
    expert_out = expert_out.reshape(dp_size, capacity, slice_width)
    returned = lax.all_to_all(expert_out, "dp", split_axis=0, concat_axis=0, tiled=True)
    picked = jnp.take(returned.reshape(experts * capacity, slice_width), slot_ids, axis=0)
    picked = picked.reshape(token_count, top_count, slice_width)
    shares = route_weights.astype(jnp.float32)
    shares = shares / jnp.sum(shares, axis=1, keepdims=True)
    mix_cols = jnp.einsum("tk,tkd->td", shares, picked.astype(jnp.float32)).astype(jnp.bfloat16)
    expert_mix = lax.all_gather(mix_cols, "tp", axis=1, tiled=True)
    attended = attend_local(
        queries, key_codes, key_scales, cache_values, new_keys, new_values, lengths
    )
    return (expert_mix, attended)


def solution(mesh):
    placed = (
        P("dp", None),
        P("dp", None),
        P("dp", None),
        P("dp", None, "tp"),
        P("dp", None, "tp"),
        P("dp", "tp", None),
        P("dp", "tp"),
        P("dp", "tp"),
        P("tp", "dp"),
        P("dp", "tp"),
        P("dp", "tp"),
        P("dp", "tp"),
        P("dp"),
    )
    return jax.shard_map(
        on_device,
        mesh=mesh,
        in_specs=placed,
        out_specs=(P("dp", None), P("dp", "tp")),
        check_vma=False,
    )
```

profile of v0, /device:TPU:8, one launch (start us, length us, event | category | flops | bytes accessed | tf_op | source)
XLA Modules:
  0.0 142.3 jit_solution(14156088460898718591)
XLA Ops:
  7.2 0.8 copy.22
  8.3 0.2 reduce_window_sum.18
  8.4 0.2 select_reduce_fusion.1
  8.7 0.1 fusion.34
  8.9 1.0 convolution_convert_fusion.1
  9.9 0.8 reshape.483
  10.7 17.4 %all-to-all-start = ((bf16[128,2,512]{2,1,0:T(2,128)(2,1)}), bf16[128,2,512]{2,1,0:T(2,128)(2,1)S(1)}, u32[]{:S(2)}, u32[]{:S(2)}) async-start(bf16[128,2,512]{2,1,0:T(2,128)(2,1)} %reshape.483), calls=%async_computation | async-start | bytes 524288 | tf_op jit(solution)/shard_map/all_to_all | solution.py:130
  28.2 0.2 reduce-window.8
  29.1 13.7 %all-to-all-done = bf16[128,2,512]{2,1,0:T(2,128)(2,1)S(1)} async-done(((bf16[128,2,512]{2,1,0:T(2,128)(2,1)}), bf16[128,2,512]{2,1,0:T(2,128)(2,1)S(1)}, u32[]{:S(2)}, u32[]{:S(2)}) %all-to-all-start) | async-done | bytes 262176 | tf_op jit(solution)/shard_map/all_to_all | solution.py:130
  42.8 0.7 copy-done.1
  43.7 0.3 multiply_bitcast_fusion
  44.1 4.8 %fusion.26 = (bf16[2048,64]{1,0:T(8,128)(2,1)S(1)}, bf16[2048,64]{1,0:T(8,128)(2,1)S(1)}) fusion(f32[2048,1,128]{2,0,1:T(8,128)S(1)} %multiply_bitcast_fusion, f32[64]{0:T(128)S(1)} %multiply_exponential_fusion, f32[2048]{0:T(1024)S(1)} %subtract_convert_fusion.1), kind=kLoop, calls=%fused_computation.38 | loop fusion | flops 1179648 | bytes 1581312 | tf_op jit(solution)/shard_map/concatenate | solution.py:20
  48.9 0.5 fusion.65
  49.4 16.5 %all-gather.3.cloned.1.call-done = bf16[512,2,512]{2,1,0:T(2,128)(2,1)} async-done(((bf16[128,2,512]{2,1,0:T(2,128)(2,1)}), bf16[512,2,512]{2,1,0:T(2,128)(2,1)}) %all-gather.3.cloned.1.call-update) | async-done | bytes 1048592 | tf_op jit(solution)/shard_map/all_gather | solution.py:131
  65.9 1.5 %reshape.484 = bf16[4,256,512]{2,1,0:T(8,128)(2,1)S(1)} reshape(bf16[512,2,512]{2,1,0:T(2,128)(2,1)} %all-gather.3.cloned.1.call-done) | data formatting | bytes 2097152 | tf_op jit(solution)/shard_map/reshape | solution.py:133
  67.4 1.7 %convolution_bitcast_fusion.1 = f32[256,256]{1,0:T(8,128)S(1)} fusion(bf16[4,256,512]{2,1,0:T(8,128)(2,1)S(1)} %reshape.484, bf16[4,512,256]{2,1,0:T(8,128)(2,1)} %bitcast.111), kind=kOutput, calls=%fused_computation.14 | convolution fusion | flops 268435456 | bytes 2359296 | tf_op jit(solution)/shard_map/tsd,tdh->sh/dot_general | solution.py:136
  69.1 3.5 %convolution_convert_fusion = bf16[256,2048]{1,0:T(8,128)(2,1)} fusion(bf16[4,256,512]{2,1,0:T(8,128)(2,1)S(1)} %reshape.484, bf16[4,512,256]{2,1,0:T(8,128)(2,1)S(1)} %bitcast.109, bf16[1,256,2048]{2,1,0:T(8,128)(2,1)} %param.18, f32[256,256]{1,0:T(8,128)S(1)} %convolution_bitcast_fusion.1), kind=kOutput, calls=%fused_computation.1 | convolution fusion | flops 537788416 | bytes 4456448 | tf_op jit(solution)/shard_map/dot_general | solution.py:139
  72.6 2.4 %copy.38 = bf16[32,4,8,512]{3,2,0,1:T(8,128)(2,1)} copy(bf16[32,4,8,512]{3,2,1,0:T(8,128)(2,1)} %bitcast.112) | data formatting | bytes 2097152 | tf_op jit(solution)/shard_map/reshape | solution.py:140
  74.9 3.5 %all-to-all-start.1 = ((bf16[256,4,512]{2,0,1:T(8,128)(2,1)}), bf16[256,4,512]{2,0,1:T(8,128)(2,1)S(1)}, u32[]{:S(2)}, u32[]{:S(2)}) async-start(bf16[256,4,512]{2,0,1:T(8,128)(2,1)} %bitcast.110), calls=%async_computation.1 | async-start | bytes 2097152 | tf_op jit(solution)/shard_map/all_to_all | solution.py:141
  78.5 0.2 fusion.47
  78.7 0.3 fusion.17
  79.0 12.9 %all-to-all-done.1 = bf16[256,4,512]{2,0,1:T(8,128)(2,1)S(1)} async-done(((bf16[256,4,512]{2,0,1:T(8,128)(2,1)}), bf16[256,4,512]{2,0,1:T(8,128)(2,1)S(1)}, u32[]{:S(2)}, u32[]{:S(2)}) %all-to-all-start.1) | async-done | bytes 1048608 | tf_op jit(solution)/shard_map/all_to_all | solution.py:141
  91.8 0.2 reduce_sum.55
  92.1 0.8 reshape.486
  92.9 14.2 %all-to-all-start.2 = ((bf16[128,2,512]{2,1,0:T(2,128)(2,1)}), bf16[128,2,512]{2,1,0:T(2,128)(2,1)S(1)}, u32[]{:S(2)}, u32[]{:S(2)}) async-start(bf16[128,2,512]{2,1,0:T(2,128)(2,1)} %reshape.486), calls=%async_computation.2 | async-start | bytes 524288 | tf_op jit(solution)/shard_map/all_to_all | solution.py:144
  107.1 0.4 fusion.11
  107.4 0.6 copy.40
  108.1 13.7 %all-to-all-done.2 = bf16[128,2,512]{2,1,0:T(2,128)(2,1)S(1)} async-done(((bf16[128,2,512]{2,1,0:T(2,128)(2,1)}), bf16[128,2,512]{2,1,0:T(2,128)(2,1)S(1)}, u32[]{:S(2)}, u32[]{:S(2)}) %all-to-all-start.2) | async-done | bytes 262176 | tf_op jit(solution)/shard_map/all_to_all | solution.py:144
  121.9 0.8 gather_fusion
  122.7 0.2 fusion.32
  123.0 11.9 %all_gather.11 = bf16[16,2048]{1,0:T(8,128)(2,1)S(1)} all-gather(bf16[16,512]{1,0:T(8,128)(2,1)S(1)} %bitcast.114), channel_id=1, replica_groups=mesh['dp'=128,'tp'=4] {'tp'}, dimensions={1}, use_global_device_ids=true | all-gather | bytes 81920 | tf_op jit(solution)/shard_map/all_gather | solution.py:150
  134.9 0.6 copy.43
  (49 shorter events, 1.4 us)
Async XLA Ops:
  7.2 61.9 %copy-start = (bf16[1,2048,256]{2,1,0:T(8,128)(2,1)S(1)}, bf16[1,2048,256]{2,1,0:T(8,128)(2,1)}, u32[]{:S(2)}) copy-start(bf16[1,2048,256]{2,1,0:T(8,128)(2,1)} %param.17) | copy-start | bytes 3145732
  7.2 21.0 %copy-start.5 = (s32[16,8]{0,1:T(8,128)S(1)}, s32[16,8]{0,1:T(8,128)}, u32[]{:S(2)}) copy-start(s32[16,8]{0,1:T(8,128)} %param.15) | copy-start | bytes 1540
  7.2 21.0 %copy-start.4 = (bf16[8,2048]{1,0:T(8,128)(2,1)S(1)}, bf16[8,2048]{1,0:T(8,128)(2,1)}, u32[]{:S(2)}) copy-start(bf16[8,2048]{1,0:T(8,128)(2,1)} %param.19) | copy-start | bytes 98308
  7.2 21.0 %copy-start.9 = (s32[8]{0:T(128)S(1)}, s32[8]{0:T(128)}, u32[]{:S(2)}) copy-start(s32[8]{0:T(128)} %param.25) | copy-start | bytes 100
  7.2 21.3 %copy-start.7 = (bf16[8,128]{1,0:T(8,128)(2,1)S(1)}, bf16[8,128]{1,0:T(8,128)(2,1)}, u32[]{:S(2)}) copy-start(bf16[8,128]{1,0:T(8,128)(2,1)} %param.23) | copy-start | bytes 6148
  7.2 21.8 %copy-start.8 = (bf16[8,128]{1,0:T(8,128)(2,1)S(1)}, bf16[8,128]{1,0:T(8,128)(2,1)}, u32[]{:S(2)}) copy-start(bf16[8,128]{1,0:T(8,128)(2,1)} %param.24) | copy-start | bytes 6148
  8.8 34.9 %copy-start.2 = (bf16[2048,128]{1,0:T(8,128)(2,1)S(1)}, bf16[2048,128]{1,0:T(8,128)(2,1)}, u32[]{:S(2)}) copy-start(bf16[2048,128]{1,0:T(8,128)(2,1)} %param.20) | copy-start | bytes 1572868
  8.9 34.9 %copy-start.6 = (f32[1,2048]{1,0:T(1,128)S(1)}, f32[1,2048]{1,0:T(1,128)}, u32[]{:S(2)}) copy-start(f32[1,2048]{1,0:T(1,128)} %param.21) | copy-start | bytes 24580
  10.7 32.1 %all-to-all-start = ((bf16[128,2,512]{2,1,0:T(2,128)(2,1)}), bf16[128,2,512]{2,1,0:T(2,128)(2,1)S(1)}, u32[]{:S(2)}, u32[]{:S(2)}) async-start(bf16[128,2,512]{2,1,0:T(2,128)(2,1)} %reshape.483), calls=%async_computation | async-start | bytes 524288 | tf_op jit(solution)/shard_map/all_to_all | solution.py:130
  28.1 37.8 %all-gather.3.cloned.1.call-start = ((), (), s32[]{:S(2)}) async-start(), calls=%async_computation.3 | async-start | bytes 1310720 | tf_op jit(solution)/shard_map/all_gather | solution.py:131
  42.8 0.7 copy-start.1
  74.9 16.9 %all-to-all-start.1 = ((bf16[256,4,512]{2,0,1:T(8,128)(2,1)}), bf16[256,4,512]{2,0,1:T(8,128)(2,1)S(1)}, u32[]{:S(2)}, u32[]{:S(2)}) async-start(bf16[256,4,512]{2,0,1:T(8,128)(2,1)} %bitcast.110), calls=%async_computation.1 | async-start | bytes 2097152 | tf_op jit(solution)/shard_map/all_to_all | solution.py:141
  92.1 15.0 %copy-start.3 = (bf16[2048,128]{1,0:T(8,128)(2,1)S(1)}, bf16[2048,128]{1,0:T(8,128)(2,1)}, u32[]{:S(2)}) copy-start(bf16[2048,128]{1,0:T(8,128)(2,1)} %param.22) | copy-start | bytes 1572868
  92.9 28.9 %all-to-all-start.2 = ((bf16[128,2,512]{2,1,0:T(2,128)(2,1)}), bf16[128,2,512]{2,1,0:T(2,128)(2,1)S(1)}, u32[]{:S(2)}, u32[]{:S(2)}) async-start(bf16[128,2,512]{2,1,0:T(2,128)(2,1)} %reshape.486), calls=%async_computation.2 | async-start | bytes 524288 | tf_op jit(solution)/shard_map/all_to_all | solution.py:144
Sparse Core Ops, SparseCore 0:
  43.7 22.2 all-gather.2
where the time goes:
time: 143 us; the launch traced here: 142 us
  waiting for transfers between devices  56.8 us (40%)
  starting transfers between devices  35.1 us (25%)
  between operations  14.4 us (10%)
  blocking collectives  11.9 us (8%)
  local copies, waits for them, and re-layouts  9.56 us (7%)
  matrix products  7.53 us (5%)
  other arithmetic  7.1 us (5%)
    all_to_all x1, starting transfers between devices, on_device(): lax.all_to_all(outgoing, 'dp', split_axis=0, concat_axis=0, tiled=True)  17.4 us
    all_gather x1, waiting for transfers between devices, on_device(): arrived = lax.all_gather(arrived, 'tp', axis=0, tiled=False)  16.5 us
    all_to_all x1, starting transfers between devices, on_device(): lax.all_to_all(expert_out, 'dp', split_axis=0, concat_axis=0, tiled=True)  14.2 us
    all_to_all x1, waiting for transfers between devices, on_device(): lax.all_to_all(outgoing, 'dp', split_axis=0, concat_axis=0, tiled=True)  13.7 us
    all_to_all x1, waiting for transfers between devices, on_device(): lax.all_to_all(expert_out, 'dp', split_axis=0, concat_axis=0, tiled=True)  13.7 us
    all_to_all x1, waiting for transfers between devices, on_device(): lax.all_to_all(partial_value, 'tp', split_axis=1, concat_axis=1, tiled=True)  12.9 us
    all_gather x1, blocking collectives, on_device(): expert_mix = lax.all_gather(mix_cols, 'tp', axis=1, tiled=True)  11.9 us
    concatenate x4, other arithmetic, rotate(): jnp.concatenate([front_half * cosine - back_half * sine_part, back_half *...  5.09 us
  transfers between devices with their start and end apart: 4, of which 4 were waited for; matrix products, arithmetic and copies ran while one was open for 6% of the time, Pallas kernels for 0%

commit v1 on v0

--- a/solution.py
+++ b/solution.py
@@ -147,7 +147,9 @@
     shares = route_weights.astype(jnp.float32)
     shares = shares / jnp.sum(shares, axis=1, keepdims=True)
     mix_cols = jnp.einsum("tk,tkd->td", shares, picked.astype(jnp.float32)).astype(jnp.bfloat16)
-    expert_mix = lax.all_gather(mix_cols, "tp", axis=1, tiled=True)
+    expert_mix = jnp.concatenate(
+        lax.all_to_all(jnp.stack([mix_cols] * lax.axis_size("tp")), "tp", 0, 0), axis=1
+    )
     attended = attend_local(
         queries, key_codes, key_scales, cache_values, new_keys, new_values, lengths
     )

time: 143 us -> 137 us (0.958)
  blocking collectives: 11.9 us -> 0 us
  waiting for transfers between devices: 56.8 us -> 60.4 us
  starting transfers between devices: 35.1 us -> 38.4 us
    all_gather x1 -> x0, blocking collectives: 11.9 us -> none  [on_device(): expert_mix = lax.all_gather(mix_cols, 'tp', axis=1, tiled=True)]
    all_to_all x0 -> x1, waiting for transfers between devices: none -> 4.59 us  [on_device(): lax.all_to_all(jnp.stack([mix_cols] * lax.axis_size('tp')), 'tp', 0, 0)]
    all_to_all x0 -> x1, starting transfers between devices: none -> 3.28 us  [on_device(): lax.all_to_all(jnp.stack([mix_cols] * lax.axis_size('tp')), 'tp', 0, 0)]
    all_to_all x1, waiting for transfers between devices: 12.9 us -> 11.3 us  [on_device(): lax.all_to_all(partial_value, 'tp', split_axis=1, concat_axis=1, tiled=True)]
  transfers between devices with their start and end apart: 4 -> 5, of which waited for: 4 -> 5; matrix products, arithmetic and copies ran while one was open for 6% -> 7% of each run, Pallas kernels for 0% -> 0%
where the time goes in v1:
time: 137 us; the launch traced here: 136 us
  waiting for transfers between devices  60.4 us (44%)
  starting transfers between devices  38.4 us (28%)
  between operations  14.4 us (11%)
  local copies, waits for them, and re-layouts  8.94 us (7%)
  other arithmetic  7.86 us (6%)
  matrix products  6.52 us (5%)
    all_to_all x1, starting transfers between devices, on_device(): lax.all_to_all(outgoing, 'dp', split_axis=0, concat_axis=0, tiled=True)  17.4 us
    all_gather x1, waiting for transfers between devices, on_device(): arrived = lax.all_gather(arrived, 'tp', axis=0, tiled=False)  16.3 us
    all_to_all x1, waiting for transfers between devices, on_device(): lax.all_to_all(expert_out, 'dp', split_axis=0, concat_axis=0, tiled=True)  14.3 us
    all_to_all x1, starting transfers between devices, on_device(): lax.all_to_all(expert_out, 'dp', split_axis=0, concat_axis=0, tiled=True)  14.2 us
    all_to_all x1, waiting for transfers between devices, on_device(): lax.all_to_all(outgoing, 'dp', split_axis=0, concat_axis=0, tiled=True)  13.8 us
    all_to_all x1, waiting for transfers between devices, on_device(): lax.all_to_all(partial_value, 'tp', split_axis=1, concat_axis=1, tiled=True)  11.3 us
    concatenate x4, other arithmetic, rotate(): jnp.concatenate([front_half * cosine - back_half * sine_part, back_half *...  5.86 us
    all_to_all x1, waiting for transfers between devices, on_device(): lax.all_to_all(jnp.stack([mix_cols] * lax.axis_size('tp')), 'tp', 0, 0)  4.59 us
  transfers between devices with their start and end apart: 5, of which 5 were waited for; matrix products, arithmetic and copies ran while one was open for 7% of the time, Pallas kernels for 0%

profile of v1, /device:TPU:8, one launch (start us, length us, event | category | flops | bytes accessed | tf_op | source)
XLA Modules:
  0.0 136.5 jit_solution(10404138661684247856)
XLA Ops:
  7.2 0.8 copy.26
  8.2 0.2 reduce_window_sum.18
  8.9 1.0 convolution_convert_fusion.1
  9.9 0.8 reshape.491
  10.7 17.4 %all-to-all-start = ((bf16[128,2,512]{2,1,0:T(2,128)(2,1)}), bf16[128,2,512]{2,1,0:T(2,128)(2,1)S(1)}, u32[]{:S(2)}, u32[]{:S(2)}) async-start(bf16[128,2,512]{2,1,0:T(2,128)(2,1)} %reshape.491), calls=%async_computation | async-start | bytes 524288 | tf_op jit(solution)/shard_map/all_to_all | solution.py:130
  28.3 0.2 reduce-window.8
  29.0 13.8 %all-to-all-done = bf16[128,2,512]{2,1,0:T(2,128)(2,1)S(1)} async-done(((bf16[128,2,512]{2,1,0:T(2,128)(2,1)}), bf16[128,2,512]{2,1,0:T(2,128)(2,1)S(1)}, u32[]{:S(2)}, u32[]{:S(2)}) %all-to-all-start) | async-done | bytes 262176 | tf_op jit(solution)/shard_map/all_to_all | solution.py:130
  42.8 0.7 copy-done.2
  43.7 0.3 multiply_bitcast_fusion
  44.0 5.6 %fusion.26 = (bf16[2048,64]{1,0:T(8,128)(2,1)}, bf16[2048,64]{1,0:T(8,128)(2,1)}) fusion(f32[2048,1,128]{2,0,1:T(8,128)S(1)} %multiply_bitcast_fusion, f32[64]{0:T(128)S(1)} %multiply_exponential_fusion, f32[2048]{0:T(1024)S(1)} %subtract_convert_fusion.1), kind=kLoop, calls=%fused_computation.38 | loop fusion | flops 1179648 | bytes 1581312 | tf_op jit(solution)/shard_map/concatenate | solution.py:20
  49.6 16.3 %all-gather.3.cloned.1.call-done = bf16[512,2,512]{2,1,0:T(2,128)(2,1)} async-done(((bf16[128,2,512]{2,1,0:T(2,128)(2,1)}), bf16[512,2,512]{2,1,0:T(2,128)(2,1)}) %all-gather.3.cloned.1.call-update) | async-done | bytes 1048592 | tf_op jit(solution)/shard_map/all_gather | solution.py:131
  65.9 1.5 %reshape.492 = bf16[4,256,512]{2,1,0:T(8,128)(2,1)S(1)} reshape(bf16[512,2,512]{2,1,0:T(2,128)(2,1)} %all-gather.3.cloned.1.call-done) | data formatting | bytes 2097152 | tf_op jit(solution)/shard_map/reshape | solution.py:133
  67.4 0.4 convolution_bitcast_fusion.1
  67.9 2.5 %convolution_convert_fusion = bf16[256,2048]{1,0:T(8,128)(2,1)S(1)} fusion(bf16[4,256,512]{2,1,0:T(8,128)(2,1)S(1)} %reshape.492, bf16[4,512,256]{2,1,0:T(8,128)(2,1)S(1)} %bitcast.112, bf16[1,256,2048]{2,1,0:T(8,128)(2,1)} %param.18, f32[256,256]{1,0:T(8,128)S(1)} %convolution_bitcast_fusion.1), kind=kOutput, calls=%fused_computation.1 | convolution fusion | flops 537788416 | bytes 4456448 | tf_op jit(solution)/shard_map/dot_general | solution.py:139
  70.4 1.1 copy.44
  71.4 3.5 %all-to-all-start.1 = ((bf16[256,4,512]{2,0,1:T(8,128)(2,1)}), bf16[256,4,512]{2,0,1:T(8,128)(2,1)S(1)}, u32[]{:S(2)}, u32[]{:S(2)}) async-start(bf16[256,4,512]{2,0,1:T(8,128)(2,1)} %bitcast.108), calls=%async_computation.1 | async-start | bytes 2097152 | tf_op jit(solution)/shard_map/all_to_all | solution.py:141
  75.0 0.2 fusion.47
  75.2 1.7 %fusion.65 = (f32[8,16]{1,0:T(8,128)S(1)}, f32[8,1,16,2048]{3,2,0,1:T(8,128)S(1)}) fusion(bf16[8,16,64]{2,1,0:T(8,128)(2,1)S(1)} %get-tuple-element.9, bf16[8,16,64]{2,1,0:T(8,128)(2,1)S(1)} %get-tuple-element.8, bf16[2048,64]{1,0:T(8,128)(2,1)} %get-tuple-element.7, bf16[2048,64]{1,0:T(8,128)(2,1)} %get-tuple-element.6, pred[8,2048]{1,0:T(8,128)(4,1)S(1)} %fusion.38), kind=kOutput, calls=%fused_computation.111 | convolution fusion | flops 69009280 | bytes 1622528 | tf_op jit(solution)/shard_map/rgqd,cgd->rgqc/dot_general | solution.py:54
  77.0 11.3 %all-to-all-done.1 = bf16[256,4,512]{2,0,1:T(8,128)(2,1)S(1)} async-done(((bf16[256,4,512]{2,0,1:T(8,128)(2,1)}), bf16[256,4,512]{2,0,1:T(8,128)(2,1)S(1)}, u32[]{:S(2)}, u32[]{:S(2)}) %all-to-all-start.1) | async-done | bytes 1048608 | tf_op jit(solution)/shard_map/all_to_all | solution.py:141
  88.3 0.2 reduce_sum.55
  88.6 0.8 reshape.494
  89.4 14.2 %all-to-all-start.2 = ((bf16[128,2,512]{2,1,0:T(2,128)(2,1)}), bf16[128,2,512]{2,1,0:T(2,128)(2,1)S(1)}, u32[]{:S(2)}, u32[]{:S(2)}) async-start(bf16[128,2,512]{2,1,0:T(2,128)(2,1)} %reshape.494), calls=%async_computation.2 | async-start | bytes 524288 | tf_op jit(solution)/shard_map/all_to_all | solution.py:144
  103.7 0.3 fusion.17
  104.0 14.3 %all-to-all-done.2 = bf16[128,2,512]{2,1,0:T(2,128)(2,1)S(1)} async-done(((bf16[128,2,512]{2,1,0:T(2,128)(2,1)}), bf16[128,2,512]{2,1,0:T(2,128)(2,1)S(1)}, u32[]{:S(2)}, u32[]{:S(2)}) %all-to-all-start.2) | async-done | bytes 262176 | tf_op jit(solution)/shard_map/all_to_all | solution.py:144
  118.4 0.8 gather_fusion
  119.2 0.2 fusion.32
  119.5 0.6 stack.2
  120.1 3.3 %all-to-all-start.3 = ((bf16[4,16,512]{2,1,0:T(8,128)(2,1)}), bf16[4,16,512]{2,1,0:T(8,128)(2,1)S(1)}, u32[]{:S(2)}, u32[]{:S(2)}) async-start(bf16[4,16,512]{2,1,0:T(8,128)(2,1)} %stack.2), calls=%async_computation.3 | async-start | bytes 131072 | tf_op jit(solution)/shard_map/all_to_all | solution.py:151
  123.4 0.4 fusion.11
  123.8 0.6 copy.46
  124.4 4.6 %all-to-all-done.3 = bf16[4,16,512]{2,1,0:T(8,128)(2,1)S(1)} async-done(((bf16[4,16,512]{2,1,0:T(8,128)(2,1)}), bf16[4,16,512]{2,1,0:T(8,128)(2,1)S(1)}, u32[]{:S(2)}, u32[]{:S(2)}) %all-to-all-start.3) | async-done | bytes 65568 | tf_op jit(solution)/shard_map/all_to_all | solution.py:151
  129.0 0.6 copy.35
  (53 shorter events, 1.6 us)
Async XLA Ops:
  7.2 60.7 %copy-start = (bf16[1,2048,256]{2,1,0:T(8,128)(2,1)S(1)}, bf16[1,2048,256]{2,1,0:T(8,128)(2,1)}, u32[]{:S(2)}) copy-start(bf16[1,2048,256]{2,1,0:T(8,128)(2,1)} %param.17) | copy-start | bytes 3145732
  7.2 21.1 %copy-start.5 = (bf16[8,2048]{1,0:T(8,128)(2,1)S(1)}, bf16[8,2048]{1,0:T(8,128)(2,1)}, u32[]{:S(2)}) copy-start(bf16[8,2048]{1,0:T(8,128)(2,1)} %param.19) | copy-start | bytes 98308
  7.2 21.1 %copy-start.10 = (s32[8]{0:T(128)S(1)}, s32[8]{0:T(128)}, u32[]{:S(2)}) copy-start(s32[8]{0:T(128)} %param.25) | copy-start | bytes 100
  7.2 21.3 %copy-start.8 = (bf16[8,128]{1,0:T(8,128)(2,1)S(1)}, bf16[8,128]{1,0:T(8,128)(2,1)}, u32[]{:S(2)}) copy-start(bf16[8,128]{1,0:T(8,128)(2,1)} %param.23) | copy-start | bytes 6148
  7.2 21.6 %copy-start.6 = (s32[16,8]{0,1:T(8,128)S(1)}, s32[16,8]{0,1:T(8,128)}, u32[]{:S(2)}) copy-start(s32[16,8]{0,1:T(8,128)} %param.15) | copy-start | bytes 1540
  8.8 34.8 %copy-start.3 = (bf16[2048,128]{1,0:T(8,128)(2,1)S(1)}, bf16[2048,128]{1,0:T(8,128)(2,1)}, u32[]{:S(2)}) copy-start(bf16[2048,128]{1,0:T(8,128)(2,1)} %param.20) | copy-start | bytes 1572868
  8.8 34.8 %copy-start.7 = (f32[1,2048]{1,0:T(1,128)S(1)}, f32[1,2048]{1,0:T(1,128)}, u32[]{:S(2)}) copy-start(f32[1,2048]{1,0:T(1,128)} %param.21) | copy-start | bytes 24580
  10.7 32.1 %all-to-all-start = ((bf16[128,2,512]{2,1,0:T(2,128)(2,1)}), bf16[128,2,512]{2,1,0:T(2,128)(2,1)S(1)}, u32[]{:S(2)}, u32[]{:S(2)}) async-start(bf16[128,2,512]{2,1,0:T(2,128)(2,1)} %reshape.491), calls=%async_computation | async-start | bytes 524288 | tf_op jit(solution)/shard_map/all_to_all | solution.py:130
  28.1 37.8 %all-gather.3.cloned.1.call-start = ((), (), s32[]{:S(2)}) async-start(), calls=%async_computation.4 | async-start | bytes 1310720 | tf_op jit(solution)/shard_map/all_gather | solution.py:131
  42.8 0.7 copy-start.2
  49.6 17.8 %copy-start.1 = (bf16[1,2048,256]{2,1,0:T(8,128)(2,1)S(1)}, bf16[1,2048,256]{2,1,0:T(8,128)(2,1)}, u32[]{:S(2)}) copy-start(bf16[1,2048,256]{2,1,0:T(8,128)(2,1)} %param.16) | copy-start | bytes 3145732
  71.4 16.9 %all-to-all-start.1 = ((bf16[256,4,512]{2,0,1:T(8,128)(2,1)}), bf16[256,4,512]{2,0,1:T(8,128)(2,1)S(1)}, u32[]{:S(2)}, u32[]{:S(2)}) async-start(bf16[256,4,512]{2,0,1:T(8,128)(2,1)} %bitcast.108), calls=%async_computation.1 | async-start | bytes 2097152 | tf_op jit(solution)/shard_map/all_to_all | solution.py:141
  77.0 26.7 %copy-start.9 = (bf16[8,128]{1,0:T(8,128)(2,1)S(1)}, bf16[8,128]{1,0:T(8,128)(2,1)}, u32[]{:S(2)}) copy-start(bf16[8,128]{1,0:T(8,128)(2,1)} %param.24) | copy-start | bytes 6148
  89.4 28.9 %all-to-all-start.2 = ((bf16[128,2,512]{2,1,0:T(2,128)(2,1)}), bf16[128,2,512]{2,1,0:T(2,128)(2,1)S(1)}, u32[]{:S(2)}, u32[]{:S(2)}) async-start(bf16[128,2,512]{2,1,0:T(2,128)(2,1)} %reshape.494), calls=%async_computation.2 | async-start | bytes 524288 | tf_op jit(solution)/shard_map/all_to_all | solution.py:144
  104.0 19.5 %copy-start.4 = (bf16[2048,128]{1,0:T(8,128)(2,1)S(1)}, bf16[2048,128]{1,0:T(8,128)(2,1)}, u32[]{:S(2)}) copy-start(bf16[2048,128]{1,0:T(8,128)(2,1)} %param.22) | copy-start | bytes 1572868
  120.1 8.9 %all-to-all-start.3 = ((bf16[4,16,512]{2,1,0:T(8,128)(2,1)}), bf16[4,16,512]{2,1,0:T(8,128)(2,1)S(1)}, u32[]{:S(2)}, u32[]{:S(2)}) async-start(bf16[4,16,512]{2,1,0:T(8,128)(2,1)} %stack.2), calls=%async_computation.3 | async-start | bytes 131072 | tf_op jit(solution)/shard_map/all_to_all | solution.py:151
Sparse Core Ops, SparseCore 0:
  43.7 22.2 all-gather.2
